TPU v7x, 32 devices: a whole 2x2x4 slice. The times are simulated.
32 devices in a mesh: req: 8 (over y, x, core), hid: 4 (over z).
Axes of the slice: x: 2, y: 2, z: 4, core: 2. Of those that a mesh axis runs over, the one named last changes fastest.
Arguments:
- hidden_in: bfloat16 [2048, 1024], P('req', 'hid'), may hold values from -6 to 6
- segments: int32 [8, 256], P('req'), may hold values from 0 to 7, never falling along the last dimension, each value on 1 to 128 neighbouring positions
- prefix_group: int32 [8, 8], P('req'), may hold values from 0 to 15
- prefix_cache: bfloat16 [16, 1024, 8, 128], P('req', None, 'hid'), may hold values from -400 to 400
- page_table: int32 [8, 2], P('req'), may hold values from 0 to 1, each once within a row
- norm_gain: float32 [1024], replicated, may hold values from 0.1 to 1.9
- w_query: bfloat16 [1024, 1024], P(None, 'hid'), may hold values from -0.1875 to 0.1875
- w_keyval: bfloat16 [1024, 1024], P(None, 'hid'), may hold values from -0.1875 to 0.1875
- w_out: bfloat16 [1024, 1024], P('hid'), may hold values from -0.1875 to 0.1875
- moe_gain: float32 [1024], replicated, may hold values from 0.1 to 1.9
- routes: int32 [2048, 8], P('req'), may hold values from 0 to 15, all different within a row; in each aligned block of 256 rows (0 to 255, 256 to 511, ...) at most 256 rows name the same one
- gates: float32 [2048, 8], P('req'), may hold values from 0.05 to 0.5
- w_gate_up: bfloat16 [16, 2, 1024, 512], P('req', None, None, 'hid'), may hold values from -0.1875 to 0.1875
- w_down: bfloat16 [16, 512, 1024], P('req', 'hid'), may hold values from -0.25 to 0.25
Outputs:
- hidden_out: bfloat16 [2048, 1024], P('req', 'hid')
- kv_pages: bfloat16 [16, 128, 8, 128], P('req', None, 'hid')
Inputs may be any that keep to these rules, and one draw needn't show every extreme that they name: `routes`: within the 256 rows of one row of the stream no expert is named by more than 256 tokens. `page_table`: each row is a permutation of 0 to 1. `segments`: segment numbers of a row never fall; each of the 8 documents has 1 to 128 tokens.
All inputs are finite; a program needn't handle non-finite values.
Results may differ from a plain program's by a relative error of at most 0.013.
Values may be sent and summed in bfloat16 or wider, within the bound.
No kernel may reach another device: no remote copies, remote signals or barrier semaphores. Data moves between devices by JAX's collectives and lax.ppermute only.
A program may use at most 128 MiB of HBM per device.

v0:
```python
import jax
import jax.numpy as jnp
from jax import lax
from jax.sharding import PartitionSpec as P

PAGE = 128
EPSILON = 1e-06
THETA = 10000.0


def rms_scale(row_data, gain_row):
    floats = row_data.astype(jnp.float32)
    mean_square = jnp.mean(floats * floats, axis=-1, keepdims=True)
    return (floats * lax.rsqrt(mean_square + EPSILON) * gain_row).astype(jnp.bfloat16)


def rotate(features, positions):
    half_dim = features.shape[-1] // 2
    frequency = THETA ** (-2.0 * jnp.arange(half_dim, dtype=jnp.float32) / features.shape[-1])
    angles = positions.astype(jnp.float32)[:, None] * frequency[None, :]
    cosine = jnp.cos(angles)[:, None, :]
    sine_part = jnp.sin(angles)[:, None, :]
    front_half = features[..., :half_dim]
    second = features[..., half_dim:]
    return jnp.concatenate(
        [front_half * cosine - second * sine_part, second * cosine + front_half * sine_part],
        axis=-1,
    )


def positions_of(segment_row, offset):
    earlier = jnp.sum((segment_row[None, :] < segment_row[:, None]).astype(jnp.int32), axis=1)
    token_index = jnp.arange(segment_row.shape[0], dtype=jnp.int32)
    return token_index - earlier + offset


def slots_of(route_rows, experts):
    flat_routes = route_rows.reshape(-1)
    onehot = (flat_routes[:, None] == jnp.arange(experts, dtype=jnp.int32)[None, :]).astype(
        jnp.int32
    )
    before = jnp.cumsum(onehot, axis=0) - onehot
    return (flat_routes, jnp.sum(before * onehot, axis=1))


def expert_rows(received, gate_up, down_proj):
    local_experts = down_proj.shape[0]
    slot_count = received.shape[1]
    model_width = received.shape[2]
    grouped = received.reshape(-1, local_experts, slot_count, model_width)
    gate_proj = jnp.einsum(
        "recd,edf->recf", grouped, gate_up[:, 0], preferred_element_type=jnp.float32
    )
    up_proj = jnp.einsum(
        "recd,edf->recf", grouped, gate_up[:, 1], preferred_element_type=jnp.float32
    )
    hidden = (jax.nn.silu(gate_proj) * up_proj).astype(jnp.bfloat16)
    produced = jnp.einsum("recf,efd->recd", hidden, down_proj, preferred_element_type=jnp.float32)
    return produced.reshape(-1, slot_count, model_width)


def shards(
    hidden_in,
    segments,
    prefix_group,
    prefix_cache,
    page_table,
    norm_gain,
    w_query,
    w_keyval,
    w_out,
    moe_gain,
    routes,
    gates,
    w_gate_up,
    w_down,
):
    req_count = lax.axis_size("req")
    whole = lax.all_gather(hidden_in, "hid", axis=1, tiled=True)
    tok_count = whole.shape[0]
    model_width = whole.shape[1]
    segment_row = segments[0]
    prefix_len = prefix_cache.shape[1]
    kv_heads = prefix_cache.shape[2]
    head_dim = prefix_cache.shape[3] // 2
    score_scale = head_dim ** (-0.5)
    normed = rms_scale(whole, norm_gain)
    position = positions_of(segment_row, prefix_len)
    projected = jnp.dot(normed, w_query, preferred_element_type=jnp.float32).reshape(
        tok_count, -1, head_dim
    )
    queries = rotate(projected, position).astype(jnp.bfloat16)
    q_groups = queries.shape[1] // kv_heads
    grouped_query = queries.reshape(tok_count, kv_heads, q_groups, head_dim)
    key_value = jnp.dot(normed, w_keyval, preferred_element_type=jnp.float32).reshape(
        tok_count, kv_heads, 2 * head_dim
    )
    key_rows = rotate(key_value[..., :head_dim], position).astype(jnp.bfloat16)
    value_rows = key_value[..., head_dim:].astype(jnp.bfloat16)
    pages = jnp.concatenate([key_rows, value_rows], axis=-1).reshape(
        -1, PAGE, kv_heads, 2 * head_dim
    )
    kv_pages = jnp.zeros_like(pages).at[page_table[0]].set(pages)
    token_index = jnp.arange(tok_count, dtype=jnp.int32)
    visible = (segment_row[None, :] == segment_row[:, None]) & (
        token_index[None, :] <= token_index[:, None]
    )
    local_scores = (
        jnp.einsum("tkgd,skd->kgts", grouped_query, key_rows, preferred_element_type=jnp.float32)
        * score_scale
    )
    local_scores = jnp.where(visible[None, None], local_scores, -jnp.inf)
    row_max = jnp.max(local_scores, axis=-1)
    numerators = jnp.exp(local_scores - row_max[..., None])
    totals = jnp.sum(numerators, axis=-1)
    weighted = jnp.einsum(
        "kgts,skd->kgtd",
        numerators.astype(jnp.bfloat16),
        value_rows,
        preferred_element_type=jnp.float32,
    )
    gathered = lax.all_gather(prefix_cache, "req", axis=0, tiled=True)
    window = tok_count // 2
    seg_count = prefix_group.shape[1]
    for seg in range(seg_count):
        start_row = jnp.minimum(jnp.sum((segment_row < seg).astype(jnp.int32)), tok_count - window)
        chosen = lax.dynamic_index_in_dim(gathered, prefix_group[0, seg], 0, keepdims=False)
        query_window = lax.dynamic_slice_in_dim(grouped_query, start_row, window, 0)
        scores = (
            jnp.einsum(
                "tkgd,skd->kgts",
                query_window,
                chosen[..., :head_dim],
                preferred_element_type=jnp.float32,
            )
            * score_scale
        )
        old_max = lax.dynamic_slice_in_dim(row_max, start_row, window, 2)
        old_total = lax.dynamic_slice_in_dim(totals, start_row, window, 2)
        old_weighted = lax.dynamic_slice_in_dim(weighted, start_row, window, 2)
        new_max = jnp.maximum(old_max, jnp.max(scores, axis=-1))
        decay_factor = jnp.exp(old_max - new_max)
        fresh = jnp.exp(scores - new_max[..., None])
        added = jnp.einsum(
            "kgts,skd->kgtd",
            fresh.astype(jnp.bfloat16),
            chosen[..., head_dim:],
            preferred_element_type=jnp.float32,
        )
        new_total = old_total * decay_factor + jnp.sum(fresh, axis=-1)
        new_weighted = old_weighted * decay_factor[..., None] + added
        inside = lax.dynamic_slice_in_dim(segment_row, start_row, window, 0) == seg
        row_max = lax.dynamic_update_slice_in_dim(
            row_max, jnp.where(inside[None, None], new_max, old_max), start_row, 2
        )
        totals = lax.dynamic_update_slice_in_dim(
            totals, jnp.where(inside[None, None], new_total, old_total), start_row, 2
        )
        weighted = lax.dynamic_update_slice_in_dim(
            weighted,
            jnp.where(inside[None, None, :, None], new_weighted, old_weighted),
            start_row,
            2,
        )
    attention = (
        (weighted / totals[..., None])
        .transpose(2, 0, 1, 3)
        .reshape(tok_count, -1)
        .astype(jnp.bfloat16)
    )
    partial_value = jnp.dot(attention, w_out, preferred_element_type=jnp.float32)
    share_width = hidden_in.shape[1]
    summed = lax.psum(partial_value.astype(jnp.bfloat16), "hid").astype(jnp.float32)
    middle = (whole.astype(jnp.float32) + summed).astype(jnp.bfloat16)
    middle_share = lax.dynamic_slice_in_dim(
        middle, lax.axis_index("hid") * share_width, share_width, 1
    )
    normed_moe = rms_scale(middle, moe_gain)
    local_experts = w_down.shape[0]
    experts = local_experts * req_count
    top_count = routes.shape[1]
    capacity = 2 * tok_count * top_count // experts
    flat_routes, slot = slots_of(routes, experts)
    target = flat_routes * capacity + slot
    token_rows = jnp.repeat(normed_moe, top_count, axis=0)
    outgoing = jnp.zeros((experts * capacity, model_width), jnp.bfloat16).at[target].set(token_rows)
    outgoing = outgoing.reshape(experts, capacity, model_width)
    partial_out = (lambda received: expert_rows(received, w_gate_up, w_down))(
        lax.all_to_all(outgoing, "req", split_axis=0, concat_axis=0, tiled=True)
    )
    reduced = lax.psum_scatter(
        partial_out.astype(jnp.bfloat16), "hid", scatter_dimension=2, tiled=True
    )
    returned = lax.all_to_all(reduced, "req", split_axis=0, concat_axis=0, tiled=True)
    picked = returned.reshape(experts * capacity, -1)[target].reshape(tok_count, top_count, -1)
    expert_sum = jnp.sum(picked.astype(jnp.float32) * gates[:, :, None], axis=1)
    hidden_out = (middle_share.astype(jnp.float32) + expert_sum).astype(jnp.bfloat16)
    return (hidden_out, kv_pages)


def solution(mesh):
    in_specs = (
        P("req", "hid"),
        P("req", None),
        P("req", None),
        P("req", None, "hid", None),
        P("req", None),
        P(),
        P(None, "hid"),
        P(None, "hid"),
        P("hid", None),
        P(),
        P("req", None),
        P("req", None),
        P("req", None, None, "hid"),
        P("req", "hid", None),
    )
    out_specs = (P("req", "hid"), P("req", None, "hid", None))
    return jax.shard_map(shards, mesh=mesh, in_specs=in_specs, out_specs=out_specs, check_vma=False)
```

profile of v0, /device:TPU:0, one launch (start us, length us, event | category | flops | bytes accessed | tf_op | source)
XLA Modules:
  0.0 529.4 jit_solution(13866989351808228242)
XLA Ops:
  7.3 2.5 copy.64
  28.5 4.5 reduce-window.6
  39.7 17.4 %all_gather.6 = bf16[256,1024]{1,0:T(8,128)(2,1)S(1)} all-gather(bf16[256,256]{1,0:T(8,128)(2,1)S(1)} %copy-done.8), channel_id=1, replica_groups=mesh['req'=8,'hid'=4] {'hid'}, dimensions={1}, use_global_device_ids=true | all-gather | bytes 655360 | tf_op jit(solution)/shard_map/all_gather | solution.py:79
  60.3 6.7 %all-gather.2.cloned.1.call-done = bf16[16,1024,2,128]{3,1,2,0:T(8,128)(2,1)} async-done(((bf16[2,1024,2,128]{3,1,2,0:T(8,128)(2,1)}), bf16[16,1024,2,128]{3,1,2,0:T(8,128)(2,1)}) %all-gather.2.cloned.1.call-update) | async-done | bytes 8388624 | tf_op jit(solution)/shard_map/all_gather | solution.py:122
  67.0 3.7 constant_dynamic-slice_fusion.8
  70.7 2.0 copy.79
  72.8 2.1 copy.77
  74.8 2.0 copy.75
  76.8 2.0 copy.73
  87.7 2.1 fusion.50
  96.1 2.1 fusion.49
  98.2 1.8 dynamic_update_slice.73
  105.1 2.1 fusion.48
  113.2 2.1 fusion.47
  121.3 2.1 fusion.46
  125.3 2.9 bitcast_reduce_fusion.2
  128.2 2.1 bitcast_reduce_fusion.1
  131.8 2.1 fusion.31
  135.2 2.1 fusion.45
  141.2 2.1 fusion.44
  149.9 44.7 %all-reduce.2.cloned.1.call-done = bf16[256,1024]{1,0:T(8,128)(2,1)} async-done(((bf16[256,1024]{1,0:T(8,128)(2,1)}), bf16[256,1024]{1,0:T(8,128)(2,1)}) %all-reduce.2.cloned.1.call-update) | async-done | bytes 524304 | tf_op jit(solution)/shard_map/psum | solution.py:173
  196.8 14.6 %scatter_custom_fusion = bf16[4096,1024]{1,0:T(8,128)(2,1)} fusion(s32[2048]{0:T(1024)S(1)} %bitcast.369, bf16[]{:T(256)} %constant.98.clone.1, bf16[256,1024]{1,0:T(8,128)(2,1)S(1)} %fusion.53), kind=kCustom, calls=%fused_computation.8 | custom fusion | bytes 8912898 | tf_op jit(solution)/shard_map/scatter | solution.py:186
  211.4 98.1 %all_to_all.10 = bf16[16,256,1024]{2,1,0:T(8,128)(2,1)S(1)} all-to-all(bf16[16,256,1024]{2,1,0:T(8,128)(2,1)} %bitcast.321), channel_id=1, replica_groups=mesh['req'=8,'hid'=4] {'req'}, dimensions={0} | all-to-all | bytes 16777216 | tf_op jit(solution)/shard_map/all_to_all | solution.py:189
  309.5 3.2 copy-done.2
  312.8 3.7 fusion.2
  316.5 12.7 %convert_bitcast_fusion = bf16[8,2,256,1024]{3,2,0,1:T(8,128)(2,1)} fusion(f32[2,8,256,128]{3,2,1,0:T(8,128)} %fusion.2, bf16[8,2,256,1024]{3,2,1,0:T(8,128)(2,1)} %bitcast.323, bf16[2,128,1024]{2,1,0:T(8,128)(2,1)S(1)} %copy-done, bf16[2,2,1024,128]{3,2,1,0:T(8,128)(2,1)S(1)} %copy-done.35), kind=kOutput, calls=%fused_computation.3 | convolution fusion | flops 2154823680 | bytes 19922944 | tf_op jit(solution)/shard_map/recf,efd->recd/dot_general | solution.py:58
  329.1 7.9 %copy.88 = bf16[8,2,256,1024]{3,2,1,0:T(8,128)(2,1)} copy(bf16[8,2,256,1024]{3,2,0,1:T(8,128)(2,1)} %convert_bitcast_fusion) | data formatting | bytes 16777216 | tf_op jit(solution)/shard_map/convert_element_type | solution.py:192
  337.1 142.7 %reduce-scatter.2.cloned.1.call-done = bf16[16,256,256]{2,1,0:T(8,128)(2,1)} async-done(((bf16[16,256,1024]{2,1,0:T(8,128)(2,1)}), bf16[16,256,256]{2,1,0:T(8,128)(2,1)}) %reduce-scatter.2.cloned.1.call-update) | async-done | bytes 2097168 | tf_op jit(solution)/shard_map/reduce_scatter | solution.py:191
  479.9 3.7 all-to-all-start.1
  486.3 23.9 %all-to-all-done.1 = bf16[16,256,256]{2,1,0:T(8,128)(2,1)S(1)} async-done(((bf16[16,256,256]{2,1,0:T(8,128)(2,1)}), bf16[16,256,256]{2,1,0:T(8,128)(2,1)S(1)}, u32[]{:S(2)}, u32[]{:S(2)}) %all-to-all-start.1) | async-done | bytes 2097184 | tf_op jit(solution)/shard_map/all_to_all | solution.py:194
  510.1 9.0 %gather_fusion = bf16[2048,256]{1,0:T(8,128)(2,1)} fusion(bf16[4096,256]{1,0:T(8,128)(2,1)S(1)} %bitcast.319, s32[2048]{0:T(1024)S(1)} %broadcast_clamp_fusion), kind=kCustom, calls=%fused_computation | custom fusion | bytes 2105344 | tf_op jit(solution)/shard_map/gather | solution.py:195
  519.1 1.9 fusion.7
  (186 shorter events, 61.4 us)
Async XLA Ops:
  7.2 309.3 %copy-start = (bf16[2,128,1024]{2,1,0:T(8,128)(2,1)S(1)}, bf16[2,128,1024]{2,1,0:T(8,128)(2,1)}, u32[]{:S(2)}) copy-start(bf16[2,128,1024]{2,1,0:T(8,128)(2,1)} %param.27) | copy-start | bytes 1572868
  7.2 2.7 copy-start.17
  7.2 13.6 %copy-start.13 = (s32[1,256]{1,0:T(1,128)S(1)}, s32[1,256]{1,0:T(1,128)}, u32[]{:S(2)}) copy-start(s32[1,256]{1,0:T(1,128)} %param.15) | copy-start | bytes 3076
  7.2 19.5 %copy-start.16 = (s32[256,8]{0,1:T(8,128)S(1)}, s32[256,8]{0,1:T(8,128)}, u32[]{:S(2)}) copy-start(s32[256,8]{0,1:T(8,128)} %param.24) | copy-start | bytes 24580
  7.2 32.5 %copy-start.8 = (bf16[256,256]{1,0:T(8,128)(2,1)S(1)}, bf16[256,256]{1,0:T(8,128)(2,1)}, u32[]{:S(2)}) copy-start(bf16[256,256]{1,0:T(8,128)(2,1)} %param.14) | copy-start | bytes 393220
  7.2 59.8 %all-gather.2.cloned.1.call-start = ((), (), s32[]{:S(2)}) async-start(), calls=%async_computation.3 | async-start | bytes 9437184 | tf_op jit(solution)/shard_map/all_gather | solution.py:122
  9.8 47.8 %copy-start.36 = (bf16[1024,256]{1,0:T(8,128)(2,1)S(1)}, bf16[1024,256]{1,0:T(8,128)(2,1)}, u32[]{:S(2)}) copy-start(bf16[1024,256]{1,0:T(8,128)(2,1)} %param.21) | copy-start | bytes 1572868
  9.8 47.8 %copy-start.38 = (f32[1024]{0:T(1024)S(1)}, f32[1024]{0:T(1024)}, u32[]{:S(2)}) copy-start(f32[1024]{0:T(1024)} %param.19) | copy-start | bytes 12292
  9.8 184.7 %all-reduce.2.cloned.1.call-start = ((), (), s32[]{:S(2)}) async-start(), calls=%async_computation.4 | async-start | bytes 1048576 | tf_op jit(solution)/shard_map/psum | solution.py:173
  26.9 31.3 %copy-start.37 = (bf16[1024,256]{1,0:T(8,128)(2,1)S(1)}, bf16[1024,256]{1,0:T(8,128)(2,1)}, u32[]{:S(2)}) copy-start(bf16[1024,256]{1,0:T(8,128)(2,1)} %param.20) | copy-start | bytes 1572868
  39.6 44.9 %copy-start.29 = (pred[128]{0:T(512)(128)(4,1)}, pred[128]{0:T(512)(128)(4,1)S(1)}, u32[]{:S(2)}) copy-start(pred[128]{0:T(512)(128)(4,1)S(1)} %get-tuple-element.68) | copy-start | bytes 388
  89.8 3.5 copy-start.27
  91.8 2.6 copy-start.28
  98.2 4.4 copy-start.25
  101.1 2.6 copy-start.26
  107.2 3.5 copy-start.23
  109.1 2.6 copy-start.24
  115.3 3.5 copy-start.21
  117.2 2.6 copy-start.22
  125.3 5.0 copy-start.20
  130.9 2.9 copy-start.18
  131.7 3.5 copy-start.1
  135.2 3.2 copy-start.32
  147.9 48.7 %copy-start.34 = (f32[1024]{0:T(1024)S(1)}, f32[1024]{0:T(1024)}, u32[]{:S(2)}) copy-start(f32[1024]{0:T(1024)} %param.23) | copy-start | bytes 12292
  149.7 330.2 %reduce-scatter.2.cloned.1.call-start = ((), (), s32[]{:S(2)}) async-start(), calls=%async_computation.5 | async-start | bytes 10485760 | tf_op jit(solution)/shard_map/reduce_scatter | solution.py:191
  211.4 101.3 %copy-start.35 = (bf16[2,2,1024,128]{3,2,1,0:T(8,128)(2,1)S(1)}, bf16[2,2,1024,128]{3,2,1,0:T(8,128)(2,1)}, u32[]{:S(2)}) copy-start(bf16[2,2,1024,128]{3,2,1,0:T(8,128)(2,1)} %param.26) | copy-start | bytes 3145732
  309.5 3.2 copy-start.2
  337.1 147.4 %copy-start.31 = (f32[256,8]{0,1:T(8,128)S(1)}, f32[256,8]{0,1:T(8,128)}, u32[]{:S(2)}) copy-start(f32[256,8]{0,1:T(8,128)} %param.25) | copy-start | bytes 24580
  337.1 147.5 %copy-start.10 = (bf16[256,2,32]{0,2,1:T(8,128)(2,1)S(1)}, bf16[256,2,32]{0,2,1:T(8,128)(2,1)}, u32[]{:S(2)}) copy-start(bf16[256,2,32]{0,2,1:T(8,128)(2,1)} %copy-done.9) | copy-start | bytes 98308
  337.1 147.5 %copy-start.12 = (bf16[256,2,32]{0,2,1:T(8,128)(2,1)S(1)}, bf16[256,2,32]{0,2,1:T(8,128)(2,1)}, u32[]{:S(2)}) copy-start(bf16[256,2,32]{0,2,1:T(8,128)(2,1)} %copy-done.11) | copy-start | bytes 98308
  337.1 147.7 %copy-start.39 = (s32[1,2]{1,0:T(1,128)S(1)}, s32[1,2]{1,0:T(1,128)}, u32[]{:S(2)}) copy-start(s32[1,2]{1,0:T(1,128)} %param.18) | copy-start | bytes 28
  479.9 30.3 %all-to-all-start.1 = ((bf16[16,256,256]{2,1,0:T(8,128)(2,1)}), bf16[16,256,256]{2,1,0:T(8,128)(2,1)S(1)}, u32[]{:S(2)}, u32[]{:S(2)}) async-start(bf16[16,256,256]{2,1,0:T(8,128)(2,1)} %reduce-scatter.2.cloned.1.call-done), calls=%async_computation.2 | async-start | bytes 4194304 | tf_op jit(solution)/shard_map/all_to_all | solution.py:194
  (12 other events, 20.0 us)
Sparse Core Ops, SparseCore 0:
  9.9 57.0 all-gather.1
  149.8 44.7 all-reduce.1
  337.2 142.6 reduce-scatter.1
where the time goes:
time: 536 us; the launch traced here: 529 us
  waiting for transfers between devices  218 us (41%)
  blocking collectives  115 us (21%)
  local copies, waits for them, and re-layouts  80.7 us (15%)
  matrix products  48.3 us (9%)
  between operations  35.4 us (7%)
  other arithmetic  27.8 us (5%)
    reduce_scatter x1, waiting for transfers between devices, shards(): lax.psum_scatter(partial_out.astype(jnp.bfloat16), 'hid', scatter_dimensi...  143 us
    all_to_all x1, blocking collectives, shards(): lax.all_to_all(outgoing, 'req', split_axis=0, concat_axis=0, tiled=True)  98.1 us
    psum x1, waiting for transfers between devices, shards(): lax.psum(partial_value.astype(jnp.bfloat16), 'hid').astype(jnp.float32)  44.7 us
    all_to_all x1, waiting for transfers between devices, shards(): lax.all_to_all(reduced, 'req', split_axis=0, concat_axis=0, tiled=True)  23.9 us
    all_gather x1, blocking collectives, shards(): whole = lax.all_gather(hidden_in, 'hid', axis=1, tiled=True)  17.4 us
    dynamic_slice x9, local copies, waits for them, and re-layouts, shards(): lax.dynamic_index_in_dim(gathered, prefix_group[0, seg], 0, keepdims=False)  16 us
    dot_general x8, matrix products, shards(): jnp.einsum('kgts,skd->kgtd', fresh.astype(jnp.bfloat16), chosen[..., head...  15.1 us
    scatter x1, local copies, waits for them, and re-layouts, shards(): jnp.zeros((experts * capacity, model_width), jnp.bfloat16).at[target]  14.6 us
  transfers between devices with their start and end apart: 4, of which 4 were waited for; matrix products, arithmetic and copies ran while one was open for 3% of the time, Pallas kernels for 0%

commit v1 on v0

--- a/solution.py
+++ b/solution.py
@@ -2,10 +2,28 @@
 import jax.numpy as jnp
 from jax import lax
 from jax.sharding import PartitionSpec as P
+from jax.lax import axis_index, ppermute, psum
 
 PAGE = 128
 EPSILON = 1e-06
 THETA = 10000.0
+
+
+def scales_feed(local, out_dim, message):
+    current_value = local.shape
+    y_new = local.reshape(
+        *current_value[:out_dim],
+        message,
+        current_value[out_dim] // message,
+        *current_value[out_dim + 1 :]
+    )
+    return jnp.moveaxis(y_new, out_dim, 0)
+
+
+def leaf_begin(chunk, axis_k):
+    chunk = jnp.moveaxis(chunk, 0, axis_k)
+    clean = chunk.shape
+    return chunk.reshape(*clean[:axis_k], clean[axis_k] * clean[axis_k + 1], *clean[axis_k + 2 :])
 
 
 def rms_scale(row_data, gain_row):
@@ -191,7 +209,22 @@
     reduced = lax.psum_scatter(
         partial_out.astype(jnp.bfloat16), "hid", scatter_dimension=2, tiled=True
     )
-    returned = lax.all_to_all(reduced, "req", split_axis=0, concat_axis=0, tiled=True)
+    extra = psum(1, axis_name="req")
+    placed = axis_index("req")
+    block_now, e_now = (extra, placed)
+    w2 = scales_feed(reduced, 0, block_now)
+    stack_in = [w2[e_now]]
+    for i0 in range(1, block_now):
+        block_next = w2[(e_now + i0) % block_now]
+        main = ppermute(
+            block_next,
+            axis_name="req",
+            perm=[(at, (at + i0) % block_now) for at in range(block_now)],
+        )
+        stack_in.append(main)
+    mid_arr = jnp.stack(stack_in, 0)
+    w2 = mid_arr[(e_now - jnp.arange(block_now)) % block_now]
+    returned = leaf_begin(w2, 0)
     picked = returned.reshape(experts * capacity, -1)[target].reshape(tok_count, top_count, -1)
     expert_sum = jnp.sum(picked.astype(jnp.float32) * gates[:, :, None], axis=1)
     hidden_out = (middle_share.astype(jnp.float32) + expert_sum).astype(jnp.bfloat16)

time: 536 us -> 546 us (1.019)
  the two profiles are of different devices: /device:TPU:0 before, /device:TPU:19 now
where the time goes in v1:
time: 546 us; the launch traced here: 539 us
  waiting for transfers between devices  210 us (38%)
  blocking collectives  112 us (21%)
  local copies, waits for them, and re-layouts  97 us (18%)
  matrix products  48.2 us (9%)
  between operations  35.5 us (7%)
  other arithmetic  27.8 us (5%)
  starting transfers between devices  7.56 us (1%)
    reduce_scatter x1, waiting for transfers between devices, shards(): lax.psum_scatter(partial_out.astype(jnp.bfloat16), 'hid', scatter_dimensi...  144 us
    all_to_all x1, blocking collectives, shards(): lax.all_to_all(outgoing, 'req', split_axis=0, concat_axis=0, tiled=True)  99.3 us
    psum x1, waiting for transfers between devices, shards(): lax.psum(partial_value.astype(jnp.bfloat16), 'hid').astype(jnp.float32)  35.8 us
    ppermute x7, waiting for transfers between devices, shards(): ppermute(block_next, axis_name='req', perm=[(at, (at + i0) % block_now) f...  20.7 us
    dynamic_slice x9, local copies, waits for them, and re-layouts, shards(): lax.dynamic_index_in_dim(gathered, prefix_group[0, seg], 0, keepdims=False)  16 us
    dot_general x8, matrix products, shards(): jnp.einsum('kgts,skd->kgtd', fresh.astype(jnp.bfloat16), chosen[..., head...  15.1 us
    scatter x1, local copies, waits for them, and re-layouts, shards(): jnp.zeros((experts * capacity, model_width), jnp.bfloat16).at[target]  14.6 us
    dot_general x8, matrix products, shards(): jnp.einsum('tkgd,skd->kgts', query_window, chosen[..., :head_dim], prefer...  14.1 us
  transfers between devices with their start and end apart: 10, of which 6 were waited for; matrix products, arithmetic and copies ran while one was open for 4% of the time, Pallas kernels for 0%

profile of v1, /device:TPU:19, one launch (start us, length us, event | category | flops | bytes accessed | tf_op | source)
XLA Modules:
  0.0 538.6 jit_solution(4998497795187786395)
XLA Ops:
  7.3 2.5 copy.64
  28.5 4.5 reduce-window.6
  39.7 12.9 %all_gather.6 = bf16[256,1024]{1,0:T(8,128)(2,1)S(1)} all-gather(bf16[256,256]{1,0:T(8,128)(2,1)S(1)} %copy-done.8), channel_id=1, replica_groups=mesh['req'=8,'hid'=4] {'hid'}, dimensions={1}, use_global_device_ids=true | all-gather | bytes 655360 | tf_op jit(solution)/shard_map/all_gather | solution.py:97
  55.8 9.9 %all-gather.2.cloned.1.call-done = bf16[16,1024,2,128]{3,1,2,0:T(8,128)(2,1)} async-done(((bf16[2,1024,2,128]{3,1,2,0:T(8,128)(2,1)}), bf16[16,1024,2,128]{3,1,2,0:T(8,128)(2,1)}) %all-gather.2.cloned.1.call-update) | async-done | bytes 8388624 | tf_op jit(solution)/shard_map/all_gather | solution.py:140
  65.7 3.7 constant_dynamic-slice_fusion.8
  69.5 2.0 copy.79
  71.5 2.1 copy.77
  73.6 2.0 copy.75
  86.5 2.1 fusion.50
  94.9 2.1 fusion.49
  104.1 2.1 fusion.48
  113.4 2.1 fusion.47
  122.7 2.1 fusion.46
  127.7 2.9 bitcast_reduce_fusion.2
  130.6 2.1 bitcast_reduce_fusion.1
  134.4 2.1 fusion.31
  137.9 2.1 fusion.45
  145.1 2.1 fusion.44
  154.7 35.8 %all-reduce.2.cloned.1.call-done = bf16[256,1024]{1,0:T(8,128)(2,1)} async-done(((bf16[256,1024]{1,0:T(8,128)(2,1)}), bf16[256,1024]{1,0:T(8,128)(2,1)}) %all-reduce.2.cloned.1.call-update) | async-done | bytes 524304 | tf_op jit(solution)/shard_map/psum | solution.py:191
  192.7 14.6 %scatter_custom_fusion = bf16[4096,1024]{1,0:T(8,128)(2,1)} fusion(s32[2048]{0:T(1024)S(1)} %bitcast.400, bf16[]{:T(256)} %constant.152.clone.1, bf16[256,1024]{1,0:T(8,128)(2,1)S(1)} %fusion.53), kind=kCustom, calls=%fused_computation.9 | custom fusion | bytes 8912898 | tf_op jit(solution)/shard_map/scatter | solution.py:204
  207.3 99.3 %all_to_all.5 = bf16[16,256,1024]{2,1,0:T(8,128)(2,1)S(1)} all-to-all(bf16[16,256,1024]{2,1,0:T(8,128)(2,1)} %bitcast.352), channel_id=1, replica_groups=mesh['req'=8,'hid'=4] {'req'}, dimensions={0} | all-to-all | bytes 16777216 | tf_op jit(solution)/shard_map/all_to_all | solution.py:207
  306.6 3.2 copy-done.2
  309.8 3.7 fusion.2
  313.5 12.7 %convert_bitcast_fusion = bf16[8,2,256,1024]{3,2,0,1:T(8,128)(2,1)} fusion(f32[2,8,256,128]{3,2,1,0:T(8,128)} %fusion.2, bf16[8,2,256,1024]{3,2,1,0:T(8,128)(2,1)} %bitcast.354, bf16[2,128,1024]{2,1,0:T(8,128)(2,1)S(1)} %copy-done, bf16[2,2,1024,128]{3,2,1,0:T(8,128)(2,1)S(1)} %copy-done.35), kind=kOutput, calls=%fused_computation.4 | convolution fusion | flops 2154823680 | bytes 19922944 | tf_op jit(solution)/shard_map/recf,efd->recd/dot_general | solution.py:76
  326.2 7.9 %copy.88 = bf16[8,2,256,1024]{3,2,1,0:T(8,128)(2,1)} copy(bf16[8,2,256,1024]{3,2,0,1:T(8,128)(2,1)} %convert_bitcast_fusion) | data formatting | bytes 16777216 | tf_op jit(solution)/shard_map/convert_element_type | solution.py:210
  334.8 144.0 %reduce-scatter.2.cloned.1.call-done = bf16[16,256,256]{2,1,0:T(8,128)(2,1)} async-done(((bf16[16,256,1024]{2,1,0:T(8,128)(2,1)}), bf16[16,256,256]{2,1,0:T(8,128)(2,1)}) %reduce-scatter.2.cloned.1.call-update) | async-done | bytes 2097168 | tf_op jit(solution)/shard_map/reduce_scatter | solution.py:209
  478.8 2.3 dynamic-slice_bitcast_fusion
  490.8 3.3 collective-permute-done.1
  496.0 11.5 %collective-permute-done.2 = bf16[2,256,256]{2,1,0:T(8,128)(2,1)S(1)} collective-permute-done((bf16[2,256,256]{2,1,0:T(8,128)(2,1)S(1)}, bf16[2,256,256]{2,1,0:T(8,128)(2,1)S(1)}, u32[]{:S(2)}, u32[]{:S(2)}) %collective-permute-start.2) | collective-permute-done | bytes 262176 | tf_op jit(solution)/shard_map/ppermute | solution.py:219
  508.2 5.9 %collective-permute-done.3 = bf16[2,256,256]{2,1,0:T(8,128)(2,1)S(1)} collective-permute-done((bf16[2,256,256]{2,1,0:T(8,128)(2,1)S(1)}, bf16[2,256,256]{2,1,0:T(8,128)(2,1)S(1)}, u32[]{:S(2)}, u32[]{:S(2)}) %collective-permute-start.3) | collective-permute-done | bytes 262176 | tf_op jit(solution)/shard_map/ppermute | solution.py:219
  517.0 2.3 gather_fusion
  519.3 9.0 %gather_fusion.1 = bf16[2048,256]{1,0:T(8,128)(2,1)} fusion(bf16[4096,256]{1,0:T(8,128)(2,1)S(1)} %bitcast.350, s32[2048]{0:T(1024)S(1)} %broadcast_clamp_fusion), kind=kCustom, calls=%fused_computation.1 | custom fusion | bytes 2105344 | tf_op jit(solution)/shard_map/gather | solution.py:228
  (209 shorter events, 86.3 us)
Async XLA Ops:
  7.2 306.3 %copy-start = (bf16[2,128,1024]{2,1,0:T(8,128)(2,1)S(1)}, bf16[2,128,1024]{2,1,0:T(8,128)(2,1)}, u32[]{:S(2)}) copy-start(bf16[2,128,1024]{2,1,0:T(8,128)(2,1)} %param.27) | copy-start | bytes 1572868
  7.2 13.6 %copy-start.13 = (s32[1,256]{1,0:T(1,128)S(1)}, s32[1,256]{1,0:T(1,128)}, u32[]{:S(2)}) copy-start(s32[1,256]{1,0:T(1,128)} %param.15) | copy-start | bytes 3076
  7.2 19.5 %copy-start.16 = (s32[256,8]{0,1:T(8,128)S(1)}, s32[256,8]{0,1:T(8,128)}, u32[]{:S(2)}) copy-start(s32[256,8]{0,1:T(8,128)} %param.24) | copy-start | bytes 24580
  7.2 32.5 %copy-start.8 = (bf16[256,256]{1,0:T(8,128)(2,1)S(1)}, bf16[256,256]{1,0:T(8,128)(2,1)}, u32[]{:S(2)}) copy-start(bf16[256,256]{1,0:T(8,128)(2,1)} %param.14) | copy-start | bytes 393220
  7.2 58.5 %all-gather.2.cloned.1.call-start = ((), (), s32[]{:S(2)}) async-start(), calls=%async_computation.2 | async-start | bytes 9437184 | tf_op jit(solution)/shard_map/all_gather | solution.py:140
  9.8 43.3 %copy-start.36 = (bf16[1024,256]{1,0:T(8,128)(2,1)S(1)}, bf16[1024,256]{1,0:T(8,128)(2,1)}, u32[]{:S(2)}) copy-start(bf16[1024,256]{1,0:T(8,128)(2,1)} %param.21) | copy-start | bytes 1572868
  9.8 43.3 %copy-start.38 = (f32[1024]{0:T(1024)S(1)}, f32[1024]{0:T(1024)}, u32[]{:S(2)}) copy-start(f32[1024]{0:T(1024)} %param.19) | copy-start | bytes 12292
  9.8 180.6 %all-reduce.2.cloned.1.call-start = ((), (), s32[]{:S(2)}) async-start(), calls=%async_computation.3 | async-start | bytes 1048576 | tf_op jit(solution)/shard_map/psum | solution.py:191
  26.9 26.8 %copy-start.37 = (bf16[1024,256]{1,0:T(8,128)(2,1)S(1)}, bf16[1024,256]{1,0:T(8,128)(2,1)}, u32[]{:S(2)}) copy-start(bf16[1024,256]{1,0:T(8,128)(2,1)} %param.20) | copy-start | bytes 1572868
  39.6 43.7 %copy-start.29 = (pred[128]{0:T(512)(128)(4,1)}, pred[128]{0:T(512)(128)(4,1)S(1)}, u32[]{:S(2)}) copy-start(pred[128]{0:T(512)(128)(4,1)S(1)} %get-tuple-element.76) | copy-start | bytes 388
  88.6 3.5 copy-start.27
  96.9 4.4 copy-start.25
  106.2 4.4 copy-start.23
  115.5 4.4 copy-start.21
  127.7 5.0 copy-start.20
  133.3 3.2 copy-start.18
  134.4 3.5 copy-start.1
  137.9 3.9 copy-start.32
  152.8 39.8 %copy-start.34 = (f32[1024]{0:T(1024)S(1)}, f32[1024]{0:T(1024)}, u32[]{:S(2)}) copy-start(f32[1024]{0:T(1024)} %param.23) | copy-start | bytes 12292
  154.5 324.2 %reduce-scatter.2.cloned.1.call-start = ((), (), s32[]{:S(2)}) async-start(), calls=%async_computation.4 | async-start | bytes 10485760 | tf_op jit(solution)/shard_map/reduce_scatter | solution.py:209
  207.3 102.5 %copy-start.35 = (bf16[2,2,1024,128]{3,2,1,0:T(8,128)(2,1)S(1)}, bf16[2,2,1024,128]{3,2,1,0:T(8,128)(2,1)}, u32[]{:S(2)}) copy-start(bf16[2,2,1024,128]{3,2,1,0:T(8,128)(2,1)} %param.26) | copy-start | bytes 3145732
  306.6 3.2 copy-start.2
  478.7 5.1 copy-start.10
  478.7 5.1 copy-start.12
  478.7 6.4 %copy-start.31 = (f32[256,8]{0,1:T(8,128)S(1)}, f32[256,8]{0,1:T(8,128)}, u32[]{:S(2)}) copy-start(f32[256,8]{0,1:T(8,128)} %param.25) | copy-start | bytes 24580
  481.1 8.1 %collective-permute-start = (bf16[2,256,256]{2,1,0:T(8,128)(2,1)S(1)}, bf16[2,256,256]{2,1,0:T(8,128)(2,1)S(1)}, u32[]{:S(2)}, u32[]{:S(2)}) collective-permute-start(bf16[2,256,256]{2,1,0:T(8,128)(2,1)S(1)} %get-tuple-element.62), channel_id=1, source_target_pairs={{0,4},{4,8},{8,12},{12,16},{16,20},{20,24},{24,28},{28,0},{1,5},{5... | collective-permute-start | bytes 786440 | tf_op jit(solution)/shard_map/ppermute | solution.py:219
  483.9 10.2 %collective-permute-start.1 = (bf16[2,256,256]{2,1,0:T(8,128)(2,1)S(1)}, bf16[2,256,256]{2,1,0:T(8,128)(2,1)S(1)}, u32[]{:S(2)}, u32[]{:S(2)}) collective-permute-start(bf16[2,256,256]{2,1,0:T(8,128)(2,1)S(1)} %get-tuple-element.61), channel_id=1, source_target_pairs={{0,8},{4,12},{8,16},{12,20},{16,24},{20,28},{24,0},{28,4},{1,9},{5... | collective-permute-start | bytes 786440 | tf_op jit(solution)/shard_map/ppermute | solution.py:219
  486.9 29.4 %collective-permute-start.6 = (bf16[2,256,256]{2,1,0:T(8,128)(2,1)S(1)}, bf16[2,256,256]{2,1,0:T(8,128)(2,1)S(1)}, u32[]{:S(2)}, u32[]{:S(2)}) collective-permute-start(bf16[2,256,256]{2,1,0:T(8,128)(2,1)S(1)} %get-tuple-element.56), channel_id=1, source_target_pairs={{0,28},{4,0},{8,4},{12,8},{16,12},{20,16},{24,20},{28,24},{1,29},{... | collective-permute-start | bytes 786440 | tf_op jit(solution)/shard_map/ppermute | solution.py:219
  486.9 28.7 %collective-permute-start.5 = (bf16[2,256,256]{2,1,0:T(8,128)(2,1)S(1)}, bf16[2,256,256]{2,1,0:T(8,128)(2,1)S(1)}, u32[]{:S(2)}, u32[]{:S(2)}) collective-permute-start(bf16[2,256,256]{2,1,0:T(8,128)(2,1)S(1)} %get-tuple-element.57), channel_id=1, source_target_pairs={{0,24},{4,28},{8,0},{12,4},{16,8},{20,12},{24,16},{28,20},{1,25},{... | collective-permute-start | bytes 786440 | tf_op jit(solution)/shard_map/ppermute | solution.py:219
  487.2 27.7 %collective-permute-start.4 = (bf16[2,256,256]{2,1,0:T(8,128)(2,1)S(1)}, bf16[2,256,256]{2,1,0:T(8,128)(2,1)S(1)}, u32[]{:S(2)}, u32[]{:S(2)}) collective-permute-start(bf16[2,256,256]{2,1,0:T(8,128)(2,1)S(1)} %get-tuple-element.58), channel_id=1, source_target_pairs={{0,20},{4,24},{8,28},{12,0},{16,4},{20,8},{24,12},{28,16},{1,21},{... | collective-permute-start | bytes 786440 | tf_op jit(solution)/shard_map/ppermute | solution.py:219
  489.2 18.3 %collective-permute-start.2 = (bf16[2,256,256]{2,1,0:T(8,128)(2,1)S(1)}, bf16[2,256,256]{2,1,0:T(8,128)(2,1)S(1)}, u32[]{:S(2)}, u32[]{:S(2)}) collective-permute-start(bf16[2,256,256]{2,1,0:T(8,128)(2,1)S(1)} %get-tuple-element.60), channel_id=1, source_target_pairs={{0,12},{4,16},{8,20},{12,24},{16,28},{20,0},{24,4},{28,8},{1,13},{... | collective-permute-start | bytes 786440 | tf_op jit(solution)/shard_map/ppermute | solution.py:219
  494.1 20.0 %collective-permute-start.3 = (bf16[2,256,256]{2,1,0:T(8,128)(2,1)S(1)}, bf16[2,256,256]{2,1,0:T(8,128)(2,1)S(1)}, u32[]{:S(2)}, u32[]{:S(2)}) collective-permute-start(bf16[2,256,256]{2,1,0:T(8,128)(2,1)S(1)} %get-tuple-element.59), channel_id=1, source_target_pairs={{0,16},{4,20},{8,24},{12,28},{16,0},{20,4},{24,8},{28,12},{1,17},{... | collective-permute-start | bytes 786440 | tf_op jit(solution)/shard_map/ppermute | solution.py:219
  (18 other events, 33.5 us)
Sparse Core Ops, SparseCore 0:
  9.9 55.7 all-gather.1
  154.6 35.7 all-reduce.1
  334.2 144.4 reduce-scatter.1
